TPU v7x, 512 devices: a whole 4x8x8 slice. The times are simulated.
512 devices in a mesh: seq: 64 (over y, z_lo, x), ch: 8 (over z_hi, core).
Axes of the slice: x: 4, y: 8, z: 8 (z_hi: 4, z_lo: 2; z = z_hi * 2 + z_lo), core: 2. Of those that a mesh axis runs over, the one named last changes fastest.
Arguments:
- inputs: bfloat16 [16384, 1024], P('seq', 'ch'), may hold values from -6 to 6
- gate_values: bfloat16 [16384, 1024], P('seq', 'ch'), may hold values from -600 to 1100
- causal_filter: bfloat16 [16384, 1024], P('seq', 'ch'), may hold values from -0.046875 to 0.046875
- anti_filter: bfloat16 [16384, 1024], P('seq', 'ch'), may hold values from -0.046875 to 0.046875
- skip_gain: float32 [1024], P('ch'), may hold values from 0.25 to 1.75
- norm_gain: float32 [1024], P('ch'), may hold values from 0.25 to 1.75
Outputs:
- mixer_out: bfloat16 [16384, 1024], P('seq', 'ch')
All inputs are finite; a program needn't handle non-finite values.
Results may differ from a plain program's by a relative error of at most 0.007.
Values may be sent and summed in bfloat16 or wider, within the bound.
No kernel may reach another device: no remote copies, remote signals or barrier semaphores. Data moves between devices by JAX's collectives and lax.ppermute only.
A program may use at most 128 MiB of HBM per device.

v0:
```python
import numpy as np
import jax
import jax.numpy as jnp
from jax import lax
from jax.sharding import PartitionSpec as P

D = 1024
HIGHEST = lax.Precision.HIGHEST


def padded(count, unit=8):
    return -(-count // unit) * unit


def inner_tables(rows_dev):
    freqs = rows_dev + 1
    fp = padded(freqs)
    f = np.arange(freqs)[:, None]
    n = np.arange(rows_dev)[None, :]
    phase = f * n % (2 * rows_dev) * (np.pi / rows_dev)
    fwd = np.zeros((2 * fp, rows_dev))
    fwd[:freqs] = np.cos(phase)
    fwd[fp : fp + freqs] = -np.sin(phase)
    t = np.arange(rows_dev)[:, None] + rows_dev
    f2 = np.arange(freqs)[None, :]
    phase2 = f2 * t % (2 * rows_dev) * (np.pi / rows_dev)
    weight = np.where((f2 == 0) | (f2 == rows_dev), 1.0, 2.0) / (2 * rows_dev)
    inv = np.zeros((rows_dev, 2 * fp))
    inv[:, :freqs] = weight * np.cos(phase2)
    inv[:, fp : fp + freqs] = -weight * np.sin(phase2)
    return (fp, fwd, inv)


def outer_tables(blocks, fp):
    size = 2 * blocks
    j = np.arange(blocks)[:, None]
    m = np.arange(size)[None, :]
    phase = 2 * np.pi * (j * m % size) / size
    fwd = np.concatenate([np.cos(phase), np.sin(phase)], axis=1)
    mi = np.arange(size)[:, None]
    i = np.arange(blocks)[None, :]
    phase_i = 2 * np.pi * (mi * i % size) / size
    cos_i = np.cos(phase_i) / size
    sin_i = np.sin(phase_i) / size
    inv_re = np.concatenate([cos_i, -sin_i], axis=0)
    inv_im = np.concatenate([sin_i, cos_i], axis=0)
    sign = np.where(np.arange(fp) % 2 == 0, 1.0, -1.0)[:, None]
    step = 2 * np.pi * np.arange(size)[None, :] / size
    shift_re = np.cos(step) + sign
    shift_im = -np.sin(step) + 0.0 * sign
    return (fwd, inv_re, inv_im, shift_re, shift_im)


def on_device(inputs, gate_values, causal_filter, anti_filter, skip_gain, norm_gain):
    rows_dev, chan_dev = inputs.shape
    blocks = lax.axis_size("seq")
    per = chan_dev // blocks
    size = 2 * blocks
    f32 = jnp.float32
    own_index = lax.axis_index("seq")
    row_ids = lax.broadcasted_iota(jnp.int32, (rows_dev, 1), 0) + own_index * rows_dev
    anti_masked = jnp.where(row_ids > 0, anti_filter, jnp.zeros_like(anti_filter))
    fp, fwd_np, inv_np = inner_tables(rows_dev)
    ofwd_np, oinv_re_np, oinv_im_np, sh_re_np, sh_im_np = outer_tables(blocks, fp)
    fwd = jnp.asarray(fwd_np, jnp.bfloat16)
    inv = jnp.asarray(inv_np, f32)
    ofwd = jnp.asarray(ofwd_np, f32)
    oinv_re = jnp.asarray(oinv_re_np, f32)
    oinv_im = jnp.asarray(oinv_im_np, f32)
    sh_re = jnp.asarray(sh_re_np, f32)
    sh_im = jnp.asarray(sh_im_np, f32)
    stacked = jnp.stack([inputs, causal_filter, anti_masked])
    send = (
        stacked.reshape(3, rows_dev, blocks, per)
        .transpose(2, 0, 3, 1)
        .reshape(blocks, 3 * per * rows_dev)
    )
    recv = lax.all_to_all(send, "seq", 0, 0, tiled=True)
    series = recv.reshape(blocks, 3 * per, rows_dev).transpose(1, 0, 2)
    spec = jnp.einsum("fn,qbn->qfb", fwd, series, preferred_element_type=f32)
    spec = spec.astype(jnp.bfloat16).astype(f32)
    z = jnp.einsum("qfb,bk->qfk", spec, ofwd, precision=HIGHEST, preferred_element_type=f32)
    z_re, z_im = (z[:, :fp], z[:, fp:])
    x_re = (z_re[..., :size] + z_im[..., size:]).reshape(3, per, fp, size)
    x_im = (z_im[..., :size] - z_re[..., size:]).reshape(3, per, fp, size)
    c_re = sh_re * x_re[1] - sh_im * x_im[1]
    c_im = sh_re * x_im[1] + sh_im * x_re[1]
    a_re = sh_re * x_re[2] - sh_im * x_im[2]
    a_im = sh_re * x_im[2] + sh_im * x_re[2]
    k_re = c_re + a_re
    k_im = c_im - a_im
    y_re = k_re * x_re[0] - k_im * x_im[0]
    y_im = k_re * x_im[0] + k_im * x_re[0]
    y_cat = jnp.concatenate([y_re, y_im], axis=-1)
    t_re = jnp.einsum("cfk,ki->cfi", y_cat, oinv_re, precision=HIGHEST, preferred_element_type=f32)
    t_im = jnp.einsum("cfk,ki->cfi", y_cat, oinv_im, precision=HIGHEST, preferred_element_type=f32)
    total = jnp.concatenate([t_re, t_im], axis=1)
    conv_t = jnp.einsum("cfi,tf->cit", total, inv, precision=HIGHEST, preferred_element_type=f32)
    back = conv_t.transpose(1, 0, 2).reshape(blocks, per * rows_dev)
    got = lax.all_to_all(back, "seq", 0, 0, tiled=True)
    convolved = got.reshape(blocks * per, rows_dev).T
    gated_mix = gate_values.astype(f32) * (convolved + skip_gain[None, :] * inputs.astype(f32))
    squares = lax.psum(jnp.sum(gated_mix * gated_mix, axis=1), "ch")
    inv_norm = lax.rsqrt(squares / D + 1e-06)
    return (norm_gain[None, :] * gated_mix * inv_norm[:, None]).astype(jnp.bfloat16)


def solution(mesh):
    placed = (P("seq", "ch"), P("seq", "ch"), P("seq", "ch"), P("seq", "ch"), P("ch"), P("ch"))
    return jax.shard_map(
        on_device, mesh=mesh, in_specs=placed, out_specs=P("seq", "ch"), check_vma=False
    )
```

profile of v0, /device:TPU:1, one launch (start us, length us, event | category | flops | bytes accessed | tf_op | source)
XLA Modules:
  0.0 74.0 jit_solution(5732633215002907503)
XLA Ops:
  0.0 1.0 %copy.23 = bf16[256,128]{0,1:T(8,128)(2,1)S(1)} copy(bf16[256,128]{1,0:T(8,128)(2,1)} %param.13) | data formatting | bytes 131072 | tf_op args[0]
  1.1 0.9 %broadcast_select_fusion = bf16[256,128]{1,0:T(8,128)(2,1)S(1)} fusion(bf16[256,128]{1,0:T(8,128)(2,1)} %param.16, pred[256]{0:T(512)(128)(4,1)S(1)} %add_compare_fusion), kind=kLoop, calls=%fused_computation.22 | loop fusion | flops 32768 | bytes 131328 | tf_op jit(solution)/shard_map/jit(_where)/select_n | solution.py:62
  2.0 0.1 copy.25
  2.2 0.9 %copy.24 = bf16[256,128]{0,1:T(8,128)(2,1)S(1)} copy(bf16[256,128]{1,0:T(8,128)(2,1)} %param.15) | data formatting | bytes 131072 | tf_op args[2]
  3.1 0.3 maximum_bitcast_fusion
  3.5 0.1 copy.26
  3.6 0.1 all_to_all.16
  3.8 0.5 broadcast.18
  4.3 1.8 %reduce.2 = bf16[64,1536]{1,0:T(8,128)(2,1)S(1)} reduce(bf16[64,1,1536]{2,1,0:T(2,128)(2,1)S(1)} %all_to_all.16, bf16[]{:T(256)} %broadcast.18), dimensions={1}, to_apply=%all_to_all.16.reduce_sub_computation | reduce | bytes 393218 | tf_op jit(solution)/shard_map/all_to_all | solution.py:78
  6.1 0.1 reshape.58
  6.1 22.8 %all_to_all.20 = bf16[64,2,768]{2,1,0:T(2,128)(2,1)S(1)} all-to-all(bf16[64,2,768]{2,1,0:T(2,128)(2,1)S(1)} %reshape.58), channel_id=1, replica_groups=mesh['seq'=64,'ch'=8] {'seq'}, dimensions={0} | all-to-all | bytes 393216 | tf_op jit(solution)/shard_map/all_to_all | solution.py:78
  28.9 0.1 reshape.59
  29.0 1.1 %reduce = bf16[64,1536]{1,0:T(8,128)(2,1)S(1)} reduce(bf16[64,1,1536]{2,1,0:T(2,128)(2,1)S(1)} %reshape.59, bf16[]{:T(256)} %constant.45), dimensions={1}, to_apply=%all_to_all.13.reduce_sub_computation | reduce | bytes 393218 | tf_op jit(solution)/shard_map/all_to_all | solution.py:78
  30.2 0.0 copy-done.1
  30.2 0.3 fusion
  30.6 0.0 copy-done.7
  30.6 1.5 %fusion.11 = f32[6,528,256]{2,1,0:T(8,128)S(1)} fusion(bf16[6,528,64]{1,2,0:T(8,128)(2,1)S(1)} %fusion, f32[64,256,1]{1,0,2:T(8,128)S(1)} %copy-done.7), kind=kOutput, calls=%fused_computation.28 | convolution fusion | flops 622854144 | bytes 3715072 | tf_op jit(solution)/shard_map/qfb,bk->qfk/dot_general | solution.py:82
  32.1 0.0 copy-start.2
  32.1 0.0 copy-start.3
  32.1 0.2 slice_add_fusion
  32.3 0.0 copy-start.5
  32.3 0.0 copy-start.4
  32.3 0.0 copy-start
  32.3 0.7 copy-done.2
  33.0 0.1 copy-done.3
  33.0 0.2 multiply_subtract_fusion
  33.2 0.0 copy-start.8
  33.2 0.0 copy-start.9
  33.3 0.1 multiply_add_fusion
  33.3 0.0 copy-done.5
  33.3 0.7 fusion.2
  34.1 0.0 copy-done.4
  34.1 0.7 fusion.1
  34.8 0.0 copy-done
  34.8 0.5 convolution_bitcast_fusion
  35.4 0.1 copy.29
  35.5 0.8 %all_to_all.17 = f32[64,1,512]{2,1,0:T(1,128)} reshape(f32[64,2,256]{2,1,0:T(2,128)S(1)} %copy.29) | data formatting | bytes 262144 | tf_op jit(solution)/shard_map/all_to_all | solution.py:100
  36.3 5.9 %all-to-all-start.1 = ((f32[64,1,512]{2,1,0:T(1,128)}), f32[64,1,512]{2,1,0:T(1,128)S(1)}, u32[]{:S(2)}, u32[]{:S(2)}) async-start(f32[64,1,512]{2,1,0:T(1,128)} %all_to_all.17), calls=%async_computation.1 | async-start | bytes 262144 | tf_op jit(solution)/shard_map/all_to_all | solution.py:100
  42.2 0.0 copy-done.6
  42.3 0.1 copy.22
  42.4 9.6 %all-to-all-done.1 = f32[64,1,512]{2,1,0:T(1,128)S(1)} async-done(((f32[64,1,512]{2,1,0:T(1,128)}), f32[64,1,512]{2,1,0:T(1,128)S(1)}, u32[]{:S(2)}, u32[]{:S(2)}) %all-to-all-start.1) | async-done | bytes 131104 | tf_op jit(solution)/shard_map/all_to_all | solution.py:100
  52.0 0.3 reduce.1
  52.3 0.0 copy-done.8
  52.4 0.1 multiply_reduce_fusion
  52.5 20.7 %psum.7 = f32[256]{0:T(256)S(1)} all-reduce(f32[256]{0:T(256)S(1)} %multiply_reduce_fusion), channel_id=1, replica_groups=mesh['seq'=64,'ch'=8] {'ch'}, use_global_device_ids=true, to_apply=%region_1.2 | all-reduce | flops 256 | bytes 2048 | tf_op jit(solution)/shard_map/psum | solution.py:103
  73.2 0.0 copy-done.9
  73.2 0.1 multiply_convert_fusion
  73.3 0.7 copy.32
  (9 shorter events, 0.1 us)
Async XLA Ops:
  0.0 30.2 %copy-start.1 = (bf16[528,256,1]{1,0,2:T(8,128)(2,1)S(1)}, bf16[528,256,1]{1,0,2:T(8,128)(2,1)}, u32[]{:S(2)}) copy-start(bf16[528,256,1]{1,0,2:T(8,128)(2,1)} %constant.40) | copy-start | bytes 811012
  0.0 30.6 %copy-start.7 = (f32[64,256,1]{1,0,2:T(8,128)S(1)}, f32[64,256,1]{1,0,2:T(8,128)}, u32[]{:S(2)}) copy-start(f32[64,256,1]{1,0,2:T(8,128)} %constant.41) | copy-start | bytes 196612
  32.1 0.9 %copy-start.2 = (f32[264,128]{1,0:T(8,128)S(1)}, f32[264,128]{1,0:T(8,128)}, u32[]{:S(2)}) copy-start(f32[264,128]{1,0:T(8,128)} %constant.38.clone) | copy-start | bytes 405508
  32.1 1.0 %copy-start.3 = (f32[264,128]{1,0:T(8,128)S(1)}, f32[264,128]{1,0:T(8,128)}, u32[]{:S(2)}) copy-start(f32[264,128]{1,0:T(8,128)} %constant.39.clone) | copy-start | bytes 405508
  32.3 1.1 %copy-start.5 = (f32[256,64,1]{0,1,2:T(8,128)S(1)}, f32[256,64,1]{0,1,2:T(8,128)}, u32[]{:S(2)}) copy-start(f32[256,64,1]{0,1,2:T(8,128)} %constant.42) | copy-start | bytes 196612
  32.3 1.8 %copy-start.4 = (f32[256,64,1]{0,1,2:T(8,128)S(1)}, f32[256,64,1]{0,1,2:T(8,128)}, u32[]{:S(2)}) copy-start(f32[256,64,1]{0,1,2:T(8,128)} %constant.43) | copy-start | bytes 196612
  32.3 2.5 %copy-start = (f32[256,528,1]{0,1,2:T(8,128)S(1)}, f32[256,528,1]{0,1,2:T(8,128)}, u32[]{:S(2)}) copy-start(f32[256,528,1]{0,1,2:T(8,128)} %constant.44) | copy-start | bytes 1622020
  33.0 9.2 %copy-start.6 = (bf16[256,128]{1,0:T(8,128)(2,1)S(1)}, bf16[256,128]{1,0:T(8,128)(2,1)}, u32[]{:S(2)}) copy-start(bf16[256,128]{1,0:T(8,128)(2,1)} %param.14) | copy-start | bytes 196612
  33.2 19.1 %copy-start.8 = (f32[128]{0:T(128)S(1)}, f32[128]{0:T(128)}, u32[]{:S(2)}) copy-start(f32[128]{0:T(128)} %param.17) | copy-start | bytes 1540
  33.2 39.9 %copy-start.9 = (f32[128]{0:T(128)S(1)}, f32[128]{0:T(128)}, u32[]{:S(2)}) copy-start(f32[128]{0:T(128)} %param.18) | copy-start | bytes 1540
  36.3 15.7 %all-to-all-start.1 = ((f32[64,1,512]{2,1,0:T(1,128)}), f32[64,1,512]{2,1,0:T(1,128)S(1)}, u32[]{:S(2)}, u32[]{:S(2)}) async-start(f32[64,1,512]{2,1,0:T(1,128)} %all_to_all.17), calls=%async_computation.1 | async-start | bytes 262144 | tf_op jit(solution)/shard_map/all_to_all | solution.py:100
where the time goes:
time: 74.3 us; the launch traced here: 74 us
  blocking collectives  43.4 us (58%)
  waiting for transfers between devices  9.63 us (13%)
  starting transfers between devices  5.94 us (8%)
  local copies, waits for them, and re-layouts  5.73 us (8%)
  other arithmetic  5.16 us (7%)
  matrix products  3.82 us (5%)
    all_to_all x1, blocking collectives, on_device(): recv = lax.all_to_all(send, 'seq', 0, 0, tiled=True)  22.8 us
    psum x1, blocking collectives, on_device(): squares = lax.psum(jnp.sum(gated_mix * gated_mix, axis=1), 'ch')  20.7 us
    all_to_all x1, waiting for transfers between devices, on_device(): got = lax.all_to_all(back, 'seq', 0, 0, tiled=True)  9.63 us
    all_to_all x1, starting transfers between devices, on_device(): got = lax.all_to_all(back, 'seq', 0, 0, tiled=True)  5.94 us
    unnamed x25, local copies, waits for them, and re-layouts  3.02 us
    all_to_all x2, other arithmetic, on_device(): recv = lax.all_to_all(send, 'seq', 0, 0, tiled=True)  2.93 us
    dot_general x1, matrix products, on_device(): jnp.einsum('qfb,bk->qfk', spec, ofwd, precision=HIGHEST, preferred_elemen...  1.49 us
  transfers between devices with their start and end apart: 1, of which 1 were waited for; matrix products, arithmetic and copies ran while one was open for 0% of the time, Pallas kernels for 0%

commit v1 on v0

--- a/solution.py
+++ b/solution.py
@@ -100,7 +100,7 @@
     got = lax.all_to_all(back, "seq", 0, 0, tiled=True)
     convolved = got.reshape(blocks * per, rows_dev).T
     gated_mix = gate_values.astype(f32) * (convolved + skip_gain[None, :] * inputs.astype(f32))
-    squares = lax.psum(jnp.sum(gated_mix * gated_mix, axis=1), "ch")
+    squares = jnp.sum(lax.all_gather(jnp.sum(gated_mix * gated_mix, axis=1), "ch"), axis=0)
     inv_norm = lax.rsqrt(squares / D + 1e-06)
     return (norm_gain[None, :] * gated_mix * inv_norm[:, None]).astype(jnp.bfloat16)
 

time: 74.3 us -> 73 us (0.983)
  blocking collectives: 43.4 us -> 42.1 us
    psum x1 -> x0, blocking collectives: 20.7 us -> none  [on_device(): squares = lax.psum(jnp.sum(gated_mix * gated_mix, axis=1), 'ch')]
    all_gather x0 -> x1, blocking collectives: none -> 19.3 us  [on_device(): lax.all_gather(jnp.sum(gated_mix * gated_mix, axis=1), 'ch')]
where the time goes in v1:
time: 73 us; the launch traced here: 72.7 us
  blocking collectives  42.1 us (58%)
  waiting for transfers between devices  9.63 us (13%)
  starting transfers between devices  5.94 us (8%)
  local copies, waits for them, and re-layouts  5.73 us (8%)
  other arithmetic  5.19 us (7%)
  matrix products  3.82 us (5%)
    all_to_all x1, blocking collectives, on_device(): recv = lax.all_to_all(send, 'seq', 0, 0, tiled=True)  22.8 us
    all_gather x1, blocking collectives, on_device(): lax.all_gather(jnp.sum(gated_mix * gated_mix, axis=1), 'ch')  19.3 us
    all_to_all x1, waiting for transfers between devices, on_device(): got = lax.all_to_all(back, 'seq', 0, 0, tiled=True)  9.63 us
    all_to_all x1, starting transfers between devices, on_device(): got = lax.all_to_all(back, 'seq', 0, 0, tiled=True)  5.94 us
    unnamed x25, local copies, waits for them, and re-layouts  3.02 us
    all_to_all x2, other arithmetic, on_device(): recv = lax.all_to_all(send, 'seq', 0, 0, tiled=True)  2.93 us
    dot_general x1, matrix products, on_device(): jnp.einsum('qfb,bk->qfk', spec, ofwd, precision=HIGHEST, preferred_elemen...  1.49 us
  transfers between devices with their start and end apart: 1, of which 1 were waited for; matrix products, arithmetic and copies ran while one was open for 0% of the time, Pallas kernels for 0%

profile of v1, /device:TPU:1, one launch (start us, length us, event | category | flops | bytes accessed | tf_op | source)
XLA Modules:
  0.0 72.7 jit_solution(17783272990708882191)
XLA Ops:
  0.0 1.0 %copy.23 = bf16[256,128]{0,1:T(8,128)(2,1)S(1)} copy(bf16[256,128]{1,0:T(8,128)(2,1)} %param.13) | data formatting | bytes 131072 | tf_op args[0]
  1.1 0.9 %broadcast_select_fusion = bf16[256,128]{1,0:T(8,128)(2,1)S(1)} fusion(bf16[256,128]{1,0:T(8,128)(2,1)} %param.16, pred[256]{0:T(512)(128)(4,1)S(1)} %add_compare_fusion), kind=kLoop, calls=%fused_computation.22 | loop fusion | flops 32768 | bytes 131328 | tf_op jit(solution)/shard_map/jit(_where)/select_n | solution.py:62
  2.0 0.1 copy.25
  2.2 0.9 %copy.24 = bf16[256,128]{0,1:T(8,128)(2,1)S(1)} copy(bf16[256,128]{1,0:T(8,128)(2,1)} %param.15) | data formatting | bytes 131072 | tf_op args[2]
  3.1 0.3 maximum_bitcast_fusion
  3.5 0.1 copy.26
  3.6 0.1 all_to_all.16
  3.8 0.5 broadcast.25
  4.3 1.8 %reduce.3 = bf16[64,1536]{1,0:T(8,128)(2,1)S(1)} reduce(bf16[64,1,1536]{2,1,0:T(2,128)(2,1)S(1)} %all_to_all.16, bf16[]{:T(256)} %broadcast.25), dimensions={1}, to_apply=%all_to_all.16.reduce_sub_computation | reduce | bytes 393218 | tf_op jit(solution)/shard_map/all_to_all | solution.py:78
  6.1 0.1 reshape.66
  6.1 22.8 %all_to_all.20 = bf16[64,2,768]{2,1,0:T(2,128)(2,1)S(1)} all-to-all(bf16[64,2,768]{2,1,0:T(2,128)(2,1)S(1)} %reshape.66), channel_id=1, replica_groups=mesh['seq'=64,'ch'=8] {'seq'}, dimensions={0} | all-to-all | bytes 393216 | tf_op jit(solution)/shard_map/all_to_all | solution.py:78
  28.9 0.1 reshape.67
  29.0 1.1 %reduce.1 = bf16[64,1536]{1,0:T(8,128)(2,1)S(1)} reduce(bf16[64,1,1536]{2,1,0:T(2,128)(2,1)S(1)} %reshape.67, bf16[]{:T(256)} %constant.45), dimensions={1}, to_apply=%all_to_all.13.reduce_sub_computation | reduce | bytes 393218 | tf_op jit(solution)/shard_map/all_to_all | solution.py:78
  30.2 0.0 copy-done.1
  30.2 0.3 fusion
  30.6 0.0 copy-done.7
  30.6 1.5 %fusion.11 = f32[6,528,256]{2,1,0:T(8,128)S(1)} fusion(bf16[6,528,64]{1,2,0:T(8,128)(2,1)S(1)} %fusion, f32[64,256,1]{1,0,2:T(8,128)S(1)} %copy-done.7), kind=kOutput, calls=%fused_computation.28 | convolution fusion | flops 622854144 | bytes 3715072 | tf_op jit(solution)/shard_map/qfb,bk->qfk/dot_general | solution.py:82
  32.1 0.0 copy-start.2
  32.1 0.0 copy-start.3
  32.1 0.2 slice_add_fusion
  32.3 0.0 copy-start.5
  32.3 0.0 copy-start.4
  32.3 0.0 copy-start
  32.3 0.7 copy-done.2
  33.0 0.1 copy-done.3
  33.0 0.2 multiply_subtract_fusion
  33.2 0.0 copy-start.8
  33.2 0.0 copy-start.9
  33.3 0.1 multiply_add_fusion
  33.3 0.0 copy-done.5
  33.3 0.7 %fusion.2 = f32[2,264,64]{1,2,0:T(8,128)S(1)} fusion(f32[256,64,1]{0,1,2:T(8,128)S(1)} %copy-done.5, f32[2,264,128]{2,1,0:T(8,128)S(1)} %multiply_add_fusion, f32[2,264,128]{2,1,0:T(8,128)S(1)} %get-tuple-element.5), kind=kOutput, calls=%fused_computation.7 | convolution fusion | flops 103944192 | bytes 741376 | tf_op jit(solution)/shard_map/cfk,ki->cfi/dot_general | solution.py:95
  34.1 0.0 copy-done.4
  34.1 0.7 %fusion.1 = f32[2,264,64]{1,2,0:T(8,128)S(1)} fusion(f32[256,64,1]{0,1,2:T(8,128)S(1)} %copy-done.4, f32[2,264,128]{2,1,0:T(8,128)S(1)} %multiply_add_fusion, f32[2,264,128]{2,1,0:T(8,128)S(1)} %get-tuple-element.5), kind=kOutput, calls=%fused_computation.6 | convolution fusion | flops 103944192 | bytes 741376 | tf_op jit(solution)/shard_map/cfk,ki->cfi/dot_general | solution.py:96
  34.8 0.0 copy-done
  34.8 0.5 convolution_bitcast_fusion
  35.4 0.1 copy.29
  35.5 0.8 %all_to_all.17 = f32[64,1,512]{2,1,0:T(1,128)} reshape(f32[64,2,256]{2,1,0:T(2,128)S(1)} %copy.29) | data formatting | bytes 262144 | tf_op jit(solution)/shard_map/all_to_all | solution.py:100
  36.3 5.9 %all-to-all-start.1 = ((f32[64,1,512]{2,1,0:T(1,128)}), f32[64,1,512]{2,1,0:T(1,128)S(1)}, u32[]{:S(2)}, u32[]{:S(2)}) async-start(f32[64,1,512]{2,1,0:T(1,128)} %all_to_all.17), calls=%async_computation.1 | async-start | bytes 262144 | tf_op jit(solution)/shard_map/all_to_all | solution.py:100
  42.2 0.0 copy-done.6
  42.3 0.1 copy.22
  42.4 9.6 %all-to-all-done.1 = f32[64,1,512]{2,1,0:T(1,128)S(1)} async-done(((f32[64,1,512]{2,1,0:T(1,128)}), f32[64,1,512]{2,1,0:T(1,128)S(1)}, u32[]{:S(2)}, u32[]{:S(2)}) %all-to-all-start.1) | async-done | bytes 131104 | tf_op jit(solution)/shard_map/all_to_all | solution.py:100
  52.0 0.3 reduce.2
  52.3 0.0 copy-done.8
  52.4 0.1 multiply_reduce_fusion
  52.5 19.3 %all-gather.1 = f32[8,1,256]{2,1,0:T(1,128)S(1)} all-gather(f32[1,1,256]{2,1,0:T(1,128)S(1)} %bitcast.40), channel_id=2, replica_groups=mesh['seq'=64,'ch'=8] {'ch'}, dimensions={0}, use_global_device_ids=true | all-gather | bytes 9216 | tf_op jit(solution)/shard_map/all_gather | solution.py:103
  71.8 0.0 copy-done.9
  71.8 0.1 multiply_convert_fusion
  72.0 0.7 %copy.32 = bf16[256,128]{1,0:T(8,128)(2,1)} copy(bf16[256,128]{0,1:T(8,128)(2,1)S(1)} %multiply_convert_fusion) | data formatting | bytes 131072 | tf_op jit(solution)/shard_map/convert_element_type | solution.py:105
  (10 shorter events, 0.2 us)
Async XLA Ops:
  0.0 30.2 %copy-start.1 = (bf16[528,256,1]{1,0,2:T(8,128)(2,1)S(1)}, bf16[528,256,1]{1,0,2:T(8,128)(2,1)}, u32[]{:S(2)}) copy-start(bf16[528,256,1]{1,0,2:T(8,128)(2,1)} %constant.40) | copy-start | bytes 811012
  0.0 30.6 %copy-start.7 = (f32[64,256,1]{1,0,2:T(8,128)S(1)}, f32[64,256,1]{1,0,2:T(8,128)}, u32[]{:S(2)}) copy-start(f32[64,256,1]{1,0,2:T(8,128)} %constant.41) | copy-start | bytes 196612
  32.1 0.9 %copy-start.2 = (f32[264,128]{1,0:T(8,128)S(1)}, f32[264,128]{1,0:T(8,128)}, u32[]{:S(2)}) copy-start(f32[264,128]{1,0:T(8,128)} %constant.38.clone) | copy-start | bytes 405508
  32.1 1.0 %copy-start.3 = (f32[264,128]{1,0:T(8,128)S(1)}, f32[264,128]{1,0:T(8,128)}, u32[]{:S(2)}) copy-start(f32[264,128]{1,0:T(8,128)} %constant.39.clone) | copy-start | bytes 405508
  32.3 1.1 %copy-start.5 = (f32[256,64,1]{0,1,2:T(8,128)S(1)}, f32[256,64,1]{0,1,2:T(8,128)}, u32[]{:S(2)}) copy-start(f32[256,64,1]{0,1,2:T(8,128)} %constant.42) | copy-start | bytes 196612
  32.3 1.8 %copy-start.4 = (f32[256,64,1]{0,1,2:T(8,128)S(1)}, f32[256,64,1]{0,1,2:T(8,128)}, u32[]{:S(2)}) copy-start(f32[256,64,1]{0,1,2:T(8,128)} %constant.43) | copy-start | bytes 196612
  32.3 2.5 %copy-start = (f32[256,528,1]{0,1,2:T(8,128)S(1)}, f32[256,528,1]{0,1,2:T(8,128)}, u32[]{:S(2)}) copy-start(f32[256,528,1]{0,1,2:T(8,128)} %constant.44) | copy-start | bytes 1622020
  33.0 9.2 %copy-start.6 = (bf16[256,128]{1,0:T(8,128)(2,1)S(1)}, bf16[256,128]{1,0:T(8,128)(2,1)}, u32[]{:S(2)}) copy-start(bf16[256,128]{1,0:T(8,128)(2,1)} %param.14) | copy-start | bytes 196612
  33.2 19.1 %copy-start.8 = (f32[128]{0:T(128)S(1)}, f32[128]{0:T(128)}, u32[]{:S(2)}) copy-start(f32[128]{0:T(128)} %param.17) | copy-start | bytes 1540
  33.2 38.6 %copy-start.9 = (f32[128]{0:T(128)S(1)}, f32[128]{0:T(128)}, u32[]{:S(2)}) copy-start(f32[128]{0:T(128)} %param.18) | copy-start | bytes 1540
  36.3 15.7 %all-to-all-start.1 = ((f32[64,1,512]{2,1,0:T(1,128)}), f32[64,1,512]{2,1,0:T(1,128)S(1)}, u32[]{:S(2)}, u32[]{:S(2)}) async-start(f32[64,1,512]{2,1,0:T(1,128)} %all_to_all.17), calls=%async_computation.1 | async-start | bytes 262144 | tf_op jit(solution)/shard_map/all_to_all | solution.py:100
